TPU v7x, 512 devices: a whole 4x8x8 slice. The times are simulated.
512 devices in a mesh: gx: 32 (over z, y_hi, core), gy: 16 (over x, y_lo).
Axes of the slice: x: 4, y: 8 (y_hi: 2, y_lo: 4; y = y_hi * 4 + y_lo), z: 8, core: 2. Of those that a mesh axis runs over, the one named last changes fastest.
Arguments:
- design: float32 [256, 128, 128], P('gx', 'gy'), may hold values from 0.06 to 0.9
- passive: int32 [256, 128, 128], P('gx', 'gy'), may hold values 0 or 1
- basis_pairs: float32 [4, 2, 3, 256, 128, 128], P(None, None, None, 'gx', 'gy'), may hold values from -6 to 6
- supports: int32 [256, 128, 128], P('gx', 'gy'), may hold values 0 or 1
- stiffness: float32 [24, 24], replicated, may hold values from -1.25 to 1.25
- mass_matrix: float32 [24, 24], replicated, may hold values from -1.25 to 1.25
- volume_fraction: float32 [64], replicated, may hold values from 0.26 to 0.36
Outputs:
- sensitivity: float32 [256, 128, 128], P('gx', 'gy')
- design_next: float32 [256, 128, 128], P('gx', 'gy')
All inputs are finite; a program needn't handle non-finite values. No bound on the sum of `passive` or of `supports` on one device may be relied on, other than what follows from the above.
Results may differ from a plain program's by a relative error of at most 0.0003.
Values sent between devices are 32-bit elements; how exact they have to be, the bound alone decides.
No kernel may reach another device: no remote copies, remote signals or barrier semaphores. Data moves between devices by JAX's collectives and lax.ppermute only.
A program may use at most 64 MiB of HBM per device.

v0:
```python
import math
import jax
import jax.numpy as jnp
from jax import lax
from jax.sharding import PartitionSpec as P

BISECT = 6
REGIONS = 64
PENALTY_SCALE = 3.0 * (1.0 - 0.001)
OMEGA_SQUARED = 0.5
MOVE_LIMIT = 0.2


def with_halo(cells, sides, width):
    for axis, dim in sides:
        count = lax.axis_size(axis)
        ends = count - 1
        head = lax.slice_in_dim(cells, 0, width, axis=dim)
        tail = lax.slice_in_dim(cells, cells.shape[dim] - width, cells.shape[dim], axis=dim)
        cells = jnp.concatenate(
            [
                lax.ppermute(tail, axis, [(i, (i + 1) % count) for i in range(ends)]),
                cells,
                lax.ppermute(head, axis, [((i + 1) % count, i) for i in range(ends)]),
            ],
            axis=dim,
        )
    return cells


def from_behind(value, axis, steps):
    count = lax.axis_size(axis)
    initial, last = (max(0, -steps), min(count, count - steps))
    return lax.ppermute(value, axis, [(source, source + steps) for source in range(initial, last)])


def filter_taps():
    tap_list = []
    for offset_x in range(-2, 3):
        for offset_y in range(-2, 3):
            for offset_z in range(-2, 3):
                weight = 3.0 - math.sqrt(
                    offset_x * offset_x + offset_y * offset_y + offset_z * offset_z
                )
                if weight > 0.0:
                    tap_list.append((offset_x, offset_y, offset_z, weight))
    return tap_list


def stencil(padded, block_shape):
    result = jnp.zeros(block_shape, jnp.float32)
    for offset_x, offset_y, offset_z, weight in filter_taps():
        result = (
            result
            + weight
            * padded[
                2 + offset_x : 2 + offset_x + block_shape[0],
                2 + offset_y : 2 + offset_y + block_shape[1],
                2 + offset_z : 2 + offset_z + block_shape[2],
            ]
        )
    return result


def element_terms(extended, stiffness, mass_matrix):
    pair_count = extended.shape[0]
    cells_x = extended.shape[3] - 1
    cells_y = extended.shape[4] - 1
    cells_z = extended.shape[5] - 1
    stiff_energy = jnp.zeros((cells_x * cells_y * cells_z,), jnp.float32)
    mass_energy = jnp.zeros((cells_x * cells_y * cells_z,), jnp.float32)
    for pair_index in range(pair_count):
        vectors = []
        for member in range(2):
            row_list = []
            for corner_x in (0, 1):
                for corner_y in (0, 1):
                    for corner_z in (0, 1):
                        for component in range(3):
                            row_list.append(
                                extended[
                                    pair_index,
                                    member,
                                    component,
                                    corner_x : corner_x + cells_x,
                                    corner_y : corner_y + cells_y,
                                    corner_z : corner_z + cells_z,
                                ].reshape(-1)
                            )
            vectors.append(jnp.stack(row_list))
        state_rows, adjoint_rows = vectors
        stiff_energy = stiff_energy + jnp.sum(
            state_rows * jnp.dot(stiffness, adjoint_rows, precision=lax.Precision.HIGHEST), axis=0
        )
        mass_energy = mass_energy + jnp.sum(
            state_rows * jnp.dot(mass_matrix, adjoint_rows, precision=lax.Precision.HIGHEST), axis=0
        )
    return (
        stiff_energy.reshape(cells_x, cells_y, cells_z),
        mass_energy.reshape(cells_x, cells_y, cells_z),
    )


def shards(design, passive, basis_pairs, supports, stiffness, mass_matrix, volume_fraction):
    block_shape = design.shape
    size_x, size_y, size_z = block_shape
    devices_x = lax.axis_size("gx")
    devices_y = lax.axis_size("gy")
    index_x = lax.axis_index("gx")
    index_y = lax.axis_index("gy")
    grid_x = size_x * devices_x
    grid_y = size_y * devices_y
    spread_x = jnp.arange(size_x + 4, dtype=jnp.int32) + index_x * size_x - 2
    spread_y = jnp.arange(size_y + 4, dtype=jnp.int32) + index_y * size_y - 2
    valid_x = ((spread_x >= 0) & (spread_x < grid_x)).astype(jnp.float32)
    valid_y = ((spread_y >= 0) & (spread_y < grid_y)).astype(jnp.float32)
    valid_z = jnp.pad(jnp.ones((size_z,), jnp.float32), 2)
    inside = valid_x[:, None, None] * valid_y[None, :, None] * valid_z[None, None, :]
    weight_sum = stencil(inside, block_shape)
    design_wide = with_halo(design, (("gx", 0), ("gy", 1)), 2)
    design_wide = jnp.pad(design_wide, ((0, 0), (0, 0), (2, 2)))
    physical = jnp.where(passive == 1, 1.0, stencil(design_wide, block_shape) / weight_sum)
    fields = basis_pairs * (1 - supports).astype(jnp.float32)
    rim_first = from_behind(fields[:, :, :, :1], "gx", -1)
    widened = jnp.concatenate([fields, rim_first], axis=3)
    rim_second = from_behind(widened[:, :, :, :, :1], "gy", -1)
    extended = jnp.concatenate([widened, rim_second], axis=4)
    extended = jnp.pad(extended, ((0, 0), (0, 0), (0, 0), (0, 0), (0, 0), (0, 1)))
    stiff_energy, mass_energy = element_terms(extended, stiffness, mass_matrix)
    raw_sensitivity = -(
        PENALTY_SCALE * physical * physical * stiff_energy - OMEGA_SQUARED * mass_energy
    )
    raw_sensitivity = jnp.where(passive == 1, 0.0, raw_sensitivity)
    scaled_wide = with_halo(raw_sensitivity / weight_sum, (("gx", 0), ("gy", 1)), 2)
    scaled_wide = jnp.pad(scaled_wide, ((0, 0), (0, 0), (2, 2)))
    sensitivity = stencil(scaled_wide, block_shape)
    benefit = jnp.maximum(-sensitivity, 0.0)
    floor_value = jnp.maximum(design - MOVE_LIMIT, 0.0)
    ceiling = jnp.minimum(design + MOVE_LIMIT, 1.0)
    band_cells = size_z // REGIONS
    target = volume_fraction * float(grid_x * grid_y * band_cells)

    def candidate(multiplier):
        per_cell = jnp.repeat(multiplier, band_cells)[None, None, :]
        trial = design * jnp.sqrt(benefit / per_cell)
        return jnp.where(passive == 1, 1.0, jnp.minimum(ceiling, jnp.maximum(floor_value, trial)))

    def region_sum(field):
        return jnp.sum(field, axis=(0, 1)).reshape(REGIONS, band_cells).sum(axis=1)

    levels = 1

    def bisect_round(round_index, bracket):
        low_end, high_end = bracket
        level_nodes = [(low_end, high_end)]
        midpoints = []
        next_nodes = []
        for node_low, node_high in level_nodes:
            middle = jnp.sqrt(node_low * node_high)
            midpoints.append(middle)
            next_nodes.append((node_low, middle))
            next_nodes.append((middle, node_high))
        partial_volumes = jnp.stack([region_sum(candidate(middle)) for middle in midpoints])
        volumes = lax.psum(partial_volumes, ("gx", "gy"))
        position = jnp.zeros((REGIONS,), jnp.int32)
        middle = jnp.sqrt(low_end * high_end)
        heap_index = position + (2**0 - 1)
        chosen = jnp.take_along_axis(volumes, heap_index[None, :], axis=0)[0]
        heavier = chosen > target
        low_end = jnp.where(heavier, middle, low_end)
        high_end = jnp.where(heavier, high_end, middle)
        return (low_end, high_end)

    start = (jnp.full((REGIONS,), 0.0001, jnp.float32), jnp.full((REGIONS,), 10000.0, jnp.float32))
    low_end, high_end = lax.fori_loop(0, BISECT // levels, bisect_round, start)
    design_next = candidate(jnp.sqrt(low_end * high_end))
    return (sensitivity, design_next)


def solution(mesh):
    placed = (
        P("gx", "gy", None),
        P("gx", "gy", None),
        P(None, None, None, "gx", "gy", None),
        P("gx", "gy", None),
        P(),
        P(),
        P(),
    )
    return jax.shard_map(
        shards,
        mesh=mesh,
        in_specs=placed,
        out_specs=(P("gx", "gy", None), P("gx", "gy", None)),
        check_vma=False,
    )
```

profile of v0, /device:TPU:1, one launch (start us, length us, event | category | flops | bytes accessed | tf_op | source)
XLA Modules:
  0.0 711.6 jit_solution(10859632898439551738)
XLA Ops:
  1.4 8.8 %collective-permute-start.1 = (f32[2,8,128]{2,1,0:T(8,128)S(1)}, f32[2,8,128]{2,1,0:T(8,128)S(1)}, u32[]{:S(2)}, u32[]{:S(2)}) collective-permute-start(f32[2,8,128]{2,1,0:T(8,128)S(1)} %get-tuple-element.311), channel_id=1, source_target_pairs={{16,0},{32,16},{48,32},{64,48},{80,64},{96,80},{112,96},{128,112},... | collective-permute-start | bytes 24584 | tf_op jit(solution)/shard_map/ppermute | solution.py:24
  10.2 2.0 collective-permute-start
  13.0 1.2 broadcast_multiply_fusion
  14.2 2.3 collective-permute-start.4
  17.5 2.3 collective-permute-start.2
  19.9 1.3 collective-permute-start.3
  21.3 3.0 collective-permute-done.3
  25.0 1.3 collective-permute-start.5
  27.0 0.8 pad_maximum_fusion.4
  28.6 5.1 collective-permute-done.5
  34.0 0.8 fusion.359
  34.8 1.0 pad_slice_fusion.79
  35.8 1.1 pad_slice_fusion.48
  36.9 0.9 fusion.355
  37.8 1.1 fusion.356
  38.9 0.9 fusion.357
  39.8 3.7 stack.27
  43.5 5.8 stack.28
  49.3 2.7 fusion.12
  52.0 1.5 fusion.8
  53.5 3.7 stack.34
  57.2 5.8 stack.33
  63.0 2.7 fusion.15
  65.7 1.5 fusion.11
  67.2 0.9 fusion.358
  68.2 0.9 pad_slice_fusion.49
  69.2 3.6 stack.30
  73.0 3.6 stack.29
  76.7 0.8 fusion.13
  77.7 0.8 fusion.9
  78.7 3.4 stack.32
  82.1 3.4 stack.31
  85.6 0.8 fusion.14
  86.5 0.8 fusion.10
  87.4 1.2 fusion.93
  88.7 8.4 %collective-permute-start.6 = (f32[2,8,128]{2,1,0:T(8,128)S(1)}, f32[2,8,128]{2,1,0:T(8,128)S(1)}, u32[]{:S(2)}, u32[]{:S(2)}) collective-permute-start(f32[2,8,128]{2,1,0:T(8,128)S(1)} %get-tuple-element.309), channel_id=1, source_target_pairs={{0,16},{16,32},{32,48},{48,64},{64,80},{80,96},{96,112},{112,128},... | collective-permute-start | bytes 24584 | tf_op jit(solution)/shard_map/ppermute | solution.py:22
  97.1 1.9 collective-permute-start.7
  99.0 6.9 collective-permute-done.7
  106.0 2.8 collective-permute-start.8
  108.7 1.3 collective-permute-start.9
  110.1 5.8 collective-permute-done.9
  116.6 594.0 %while.13 = (s32[]{:T(128)}, f32[64]{0:T(128)S(1)}, f32[64]{0:T(128)S(1)}, s32[8,8,128]{2,1,0:T(8,128)S(1)}, f32[8,8,128]{2,1,0:T(8,128)S(1)}, /*index=5*/f32[8,...) while((s32[]{:T(128)}, f32[64]{0:T(128)S(1)}, ...), condition=%wide.region_12.13_spmd.clone, body=%wide.region_8.12_spmd.clone.sunk | while | flops 57923 | bytes 172676 | solution.py:175
  117.2 111.4 %psum.9 = f32[1,64]{1,0:T(1,128)S(1)} all-reduce(f32[1,64]{1,0:T(1,128)S(1)} %bitcast.455), channel_id=1, replica_groups=mesh['gx'=32,'gy'=16] {'gx','gy'}, use_global_device_ids=true, to_apply=%region_11.11 | all-reduce | flops 64 | bytes 512 | tf_op jit(solution)/shard_map/while/body/eval_jaxpr/psum | solution.py:164
  230.0 95.1 %psum.9 = f32[1,64]{1,0:T(1,128)S(1)} all-reduce(f32[1,64]{1,0:T(1,128)S(1)} %bitcast.455), channel_id=1, replica_groups=mesh['gx'=32,'gy'=16] {'gx','gy'}, use_global_device_ids=true, to_apply=%region_11.11 | all-reduce | flops 64 | bytes 512 | tf_op jit(solution)/shard_map/while/body/eval_jaxpr/psum | solution.py:164
  326.4 94.7 %psum.9 = f32[1,64]{1,0:T(1,128)S(1)} all-reduce(f32[1,64]{1,0:T(1,128)S(1)} %bitcast.455), channel_id=1, replica_groups=mesh['gx'=32,'gy'=16] {'gx','gy'}, use_global_device_ids=true, to_apply=%region_11.11 | all-reduce | flops 64 | bytes 512 | tf_op jit(solution)/shard_map/while/body/eval_jaxpr/psum | solution.py:164
  422.4 95.0 %psum.9 = f32[1,64]{1,0:T(1,128)S(1)} all-reduce(f32[1,64]{1,0:T(1,128)S(1)} %bitcast.455), channel_id=1, replica_groups=mesh['gx'=32,'gy'=16] {'gx','gy'}, use_global_device_ids=true, to_apply=%region_11.11 | all-reduce | flops 64 | bytes 512 | tf_op jit(solution)/shard_map/while/body/eval_jaxpr/psum | solution.py:164
  518.8 94.7 %psum.9 = f32[1,64]{1,0:T(1,128)S(1)} all-reduce(f32[1,64]{1,0:T(1,128)S(1)} %bitcast.455), channel_id=1, replica_groups=mesh['gx'=32,'gy'=16] {'gx','gy'}, use_global_device_ids=true, to_apply=%region_11.11 | all-reduce | flops 64 | bytes 512 | tf_op jit(solution)/shard_map/while/body/eval_jaxpr/psum | solution.py:164
  614.9 95.0 %psum.9 = f32[1,64]{1,0:T(1,128)S(1)} all-reduce(f32[1,64]{1,0:T(1,128)S(1)} %bitcast.455), channel_id=1, replica_groups=mesh['gx'=32,'gy'=16] {'gx','gy'}, use_global_device_ids=true, to_apply=%region_11.11 | all-reduce | flops 64 | bytes 512 | tf_op jit(solution)/shard_map/while/body/eval_jaxpr/psum | solution.py:164
  (208 shorter events, 14.6 us)
Async XLA Ops:
  0.6 48.7 %copy-start = (f32[24,24]{1,0:T(8,128)S(1)}, f32[24,24]{1,0:T(8,128)}, u32[]{:S(2)}) copy-start(f32[24,24]{1,0:T(8,128)} %param.14) | copy-start | bytes 6916
  0.6 16.8 %copy-start.3 = (f32[8,8,128]{2,1,0:T(8,128)S(1)}, f32[8,8,128]{2,1,0:T(8,128)}, u32[]{:S(2)}) copy-start(f32[8,8,128]{2,1,0:T(8,128)} %param.9) | copy-start | bytes 98308
  1.4 16.1 %collective-permute-start.1 = (f32[2,8,128]{2,1,0:T(8,128)S(1)}, f32[2,8,128]{2,1,0:T(8,128)S(1)}, u32[]{:S(2)}, u32[]{:S(2)}) collective-permute-start(f32[2,8,128]{2,1,0:T(8,128)S(1)} %get-tuple-element.311), channel_id=1, source_target_pairs={{16,0},{32,16},{48,32},{64,48},{80,64},{96,80},{112,96},{128,112},... | collective-permute-start | bytes 24584 | tf_op jit(solution)/shard_map/ppermute | solution.py:24
  10.2 7.3 %collective-permute-start = (f32[2,8,128]{2,1,0:T(8,128)S(1)}, f32[2,8,128]{2,1,0:T(8,128)S(1)}, u32[]{:S(2)}, u32[]{:S(2)}) collective-permute-start(f32[2,8,128]{2,1,0:T(8,128)S(1)} %get-tuple-element.312), channel_id=1, source_target_pairs={{0,16},{16,32},{32,48},{48,64},{64,80},{80,96},{96,112},{112,128},... | collective-permute-start | bytes 24584 | tf_op jit(solution)/shard_map/ppermute | solution.py:22
  14.2 10.3 %collective-permute-start.4 = (f32[4,2,3,1,8,128]{5,4,3,2,1,0:T(8,128)S(1)}, f32[4,2,3,1,8,128]{5,4,3,2,1,0:T(8,128)S(1)}, u32[]{:S(2)}, u32[]{:S(2)}) collective-permute-start(f32[4,2,3,1,8,128]{5,4,3,2,1,0:T(8,128)S(1)} %slice.2402), channel_id=1, source_target_pairs={{16,0},{32,16},{48,32},{64,48},{80,64},{96,80},{112,96},{128,112},... | collective-permute-start | bytes 294920 | tf_op jit(solution)/shard_map/ppermute | solution.py:34
  17.5 3.7 collective-permute-start.2
  19.9 4.5 collective-permute-start.3
  21.3 3.2 copy-start.53
  25.0 8.7 %collective-permute-start.5 = (f32[4,2,3,9,1,128]{5,3,4,2,1,0:T(8,128)S(1)}, f32[4,2,3,9,1,128]{5,3,4,2,1,0:T(8,128)S(1)}, u32[]{:S(2)}, u32[]{:S(2)}) collective-permute-start(f32[4,2,3,9,1,128]{5,3,4,2,1,0:T(8,128)S(1)} %copy.107), channel_id=1, source_target_pairs={{1,0},{2,1},{3,2},{4,3},{5,4},{6,5},{7,6},{8,7},{9,8},{10,9},{11,1... | collective-permute-start | bytes 331784 | tf_op jit(solution)/shard_map/ppermute | solution.py:34
  43.5 8.5 %copy-start.5 = (f32[24,24]{1,0:T(8,128)S(1)}, f32[24,24]{1,0:T(8,128)}, u32[]{:S(2)}) copy-start(f32[24,24]{1,0:T(8,128)} %param.13) | copy-start | bytes 6916
  49.3 2.7 copy-start.1
  63.0 2.7 copy-start.2
  67.1 2.0 copy-start.24
  67.1 2.0 copy-start.28
  67.2 2.0 copy-start.29
  67.2 2.0 copy-start.32
  68.1 4.7 copy-start.13
  68.1 4.8 copy-start.14
  68.1 4.8 copy-start.15
  68.1 4.8 copy-start.16
  68.1 4.8 copy-start.17
  68.1 4.8 copy-start.18
  68.1 4.8 copy-start.19
  68.1 4.8 copy-start.20
  68.1 4.8 copy-start.21
  68.1 4.8 copy-start.22
  68.1 4.8 copy-start.23
  69.1 3.8 copy-start.46
  69.1 3.9 copy-start.47
  69.1 3.9 copy-start.48
  69.1 3.9 copy-start.49
  69.1 3.9 copy-start.50
  69.1 3.9 copy-start.51
  76.6 1.9 copy-start.6
  76.6 1.9 copy-start.7
  77.6 4.5 copy-start.34
  77.6 4.5 copy-start.35
  77.6 4.5 copy-start.36
  77.6 4.5 copy-start.40
  77.6 4.5 copy-start.41
  77.6 4.5 copy-start.42
  77.6 4.5 copy-start.52
  87.4 22.6 %copy-start.57 = (f32[64]{0:T(128)S(1)}, f32[64]{0:T(128)}, u32[]{:S(2)}) copy-start(f32[64]{0:T(128)} %param.15) | copy-start | bytes 772
  88.7 10.3 %collective-permute-start.6 = (f32[2,8,128]{2,1,0:T(8,128)S(1)}, f32[2,8,128]{2,1,0:T(8,128)S(1)}, u32[]{:S(2)}, u32[]{:S(2)}) collective-permute-start(f32[2,8,128]{2,1,0:T(8,128)S(1)} %get-tuple-element.309), channel_id=1, source_target_pairs={{0,16},{16,32},{32,48},{48,64},{64,80},{80,96},{96,112},{112,128},... | collective-permute-start | bytes 24584 | tf_op jit(solution)/shard_map/ppermute | solution.py:22
  97.1 8.9 %collective-permute-start.7 = (f32[2,8,128]{2,1,0:T(8,128)S(1)}, f32[2,8,128]{2,1,0:T(8,128)S(1)}, u32[]{:S(2)}, u32[]{:S(2)}) collective-permute-start(f32[2,8,128]{2,1,0:T(8,128)S(1)} %get-tuple-element.310), channel_id=1, source_target_pairs={{16,0},{32,16},{48,32},{64,48},{80,64},{96,80},{112,96},{128,112},... | collective-permute-start | bytes 24584 | tf_op jit(solution)/shard_map/ppermute | solution.py:24
  106.0 4.1 collective-permute-start.8
  108.7 7.1 %collective-permute-start.9 = (f32[12,2,128]{2,1,0:T(2,128)S(1)}, f32[12,2,128]{2,1,0:T(2,128)S(1)}, u32[]{:S(2)}, u32[]{:S(2)}) collective-permute-start(f32[12,2,128]{2,1,0:T(2,128)S(1)} %get-tuple-element.301), channel_id=1, source_target_pairs={{1,0},{2,1},{3,2},{4,3},{5,4},{6,5},{7,6},{8,7},{9,8},{10,9},{11,1... | collective-permute-start | bytes 36872 | tf_op jit(solution)/shard_map/ppermute | solution.py:24
  116.6 594.3 %copy-start.33 = (f32[8,8,128]{2,1,0:T(8,128)}, f32[8,8,128]{2,1,0:T(8,128)S(1)}, u32[]{:S(2)}) copy-start(f32[8,8,128]{2,1,0:T(8,128)S(1)} %get-tuple-element.101) | copy-start | bytes 98308
  (20 other events, 36.2 us)
where the time goes:
time: 714 us; the launch traced here: 712 us
  blocking collectives  586 us (82%)
  local copies, waits for them, and re-layouts  50.1 us (7%)
  starting transfers between devices  32.4 us (5%)
  waiting for transfers between devices  20.9 us (3%)
  matrix products  11.6 us (2%)
  other arithmetic  8.48 us (1%)
    psum x6, blocking collectives, bisect_round(): volumes = lax.psum(partial_volumes, ('gx', 'gy'))  586 us
    another operation x8, local copies, waits for them, and re-layouts, element_terms(): vectors.append(jnp.stack(row_list))  33.2 us
    ppermute x4, waiting for transfers between devices, with_halo(): lax.ppermute(head, axis, [((i + 1) % count, i) for i in range(ends)])  15.8 us
    ppermute x4, starting transfers between devices, with_halo(): lax.ppermute(tail, axis, [(i, (i + 1) % count) for i in range(ends)])  15.5 us
  transfers between devices with their start and end apart: 10, of which 4 were waited for; matrix products, arithmetic and copies ran while one was open for 1% of the time, Pallas kernels for 0%

commit v1 on v0

--- a/solution.py
+++ b/solution.py
@@ -161,7 +161,7 @@
             next_nodes.append((node_low, middle))
             next_nodes.append((middle, node_high))
         partial_volumes = jnp.stack([region_sum(candidate(middle)) for middle in midpoints])
-        volumes = lax.psum(partial_volumes, ("gx", "gy"))
+        volumes = jnp.sum(lax.all_gather(partial_volumes, ("gx", "gy")), axis=0)
         position = jnp.zeros((REGIONS,), jnp.int32)
         middle = jnp.sqrt(low_end * high_end)
         heap_index = position + (2**0 - 1)

time: 714 us -> 1730 us (2.42)
  waiting for transfers between devices: 20.9 us -> 1590 us
  blocking collectives: 586 us -> 0 us
    while x0 -> x12, waiting for transfers between devices: none -> 1570 us
    psum x6 -> x0, blocking collectives: 586 us -> none  [bisect_round(): volumes = lax.psum(partial_volumes, ('gx', 'gy'))]
  transfers between devices with their start and end apart: 10 -> 16, of which waited for: 4 -> 10; matrix products, arithmetic and copies ran while one was open for 1% -> 0% of each run, Pallas kernels for 0% -> 0%
where the time goes in v1:
time: 1730 us
  waiting for transfers between devices  1590 us (92%)
  local copies, waits for them, and re-layouts  61.6 us (4%)
  starting transfers between devices  32.6 us (2%)
    while x12, waiting for transfers between devices  1570 us
  transfers between devices with their start and end apart: 16, of which 10 were waited for; matrix products, arithmetic and copies ran while one was open for 0% of the time, Pallas kernels for 0%

profile of v1, /device:TPU:1, one launch (start us, length us, event | category | flops | bytes accessed | tf_op | source)
XLA Modules:
  0.0 1725.4 jit_solution(15887802011969009662)
XLA Ops:
  8.0 8.8 collective-permute-start.1
  16.7 2.0 collective-permute-start
  19.5 1.2 broadcast_multiply_fusion
  20.7 2.3 collective-permute-start.4
  24.1 2.3 collective-permute-start.2
  26.4 1.3 collective-permute-start.3
  27.8 3.0 collective-permute-done.3
  31.5 1.3 collective-permute-start.5
  35.1 5.2 collective-permute-done.5
  41.3 1.0 pad_slice_fusion.79
  42.3 1.0 pad_slice_fusion.48
  43.4 0.9 fusion.355
  44.3 1.0 fusion.356
  45.3 0.9 fusion.357
  46.2 3.7 stack.27
  49.9 5.8 stack.28
  55.8 2.7 fusion.12
  58.4 1.5 fusion.8
  59.9 3.7 stack.34
  63.6 5.8 stack.33
  69.4 2.7 fusion.15
  72.1 1.5 fusion.11
  74.5 0.9 pad_slice_fusion.49
  75.4 3.6 stack.30
  79.3 3.6 stack.29
  84.0 0.8 fusion.9
  84.9 3.4 stack.32
  88.4 3.4 stack.31
  93.7 1.2 fusion.93
  95.0 8.4 collective-permute-start.6
  103.4 1.9 collective-permute-start.7
  105.3 6.9 collective-permute-done.7
  112.3 2.8 collective-permute-start.8
  115.0 1.3 collective-permute-start.9
  116.4 5.8 collective-permute-done.9
  122.9 1594.7 %while.13 = (s32[]{:T(128)}, f32[64]{0:T(128)S(1)}, f32[64]{0:T(128)S(1)}, s32[8,8,128]{2,1,0:T(8,128)S(1)}, f32[8,8,128]{2,1,0:T(8,128)S(1)}, /*index=5*/f32[8,...) while((s32[]{:T(128)}, f32[64]{0:T(128)S(1)}, ...), condition=%wide.region_12.13_spmd.clone, body=%wide.region_8.12_spmd.clone.sunk | while | flops 123334 | bytes 2008072 | solution.py:175
  124.5 277.1 %all-reduce.10.cloned.1.call-done = f32[32768]{0:T(1024)} async-done(((f32[32768]{0:T(1024)}), f32[32768]{0:T(1024)}) %all-reduce.10.cloned.1.call-update) | async-done | bytes 131088 | tf_op jit(solution)/shard_map/while
  401.7 1.0 reshape.118
  405.1 259.5 %all-reduce.10.cloned.1.call-done = f32[32768]{0:T(1024)} async-done(((f32[32768]{0:T(1024)}), f32[32768]{0:T(1024)}) %all-reduce.10.cloned.1.call-update) | async-done | bytes 131088 | tf_op jit(solution)/shard_map/while
  664.7 1.0 reshape.118
  668.1 259.5 %all-reduce.10.cloned.1.call-done = f32[32768]{0:T(1024)} async-done(((f32[32768]{0:T(1024)}), f32[32768]{0:T(1024)}) %all-reduce.10.cloned.1.call-update) | async-done | bytes 131088 | tf_op jit(solution)/shard_map/while
  927.7 1.0 reshape.118
  931.1 259.2 %all-reduce.10.cloned.1.call-done = f32[32768]{0:T(1024)} async-done(((f32[32768]{0:T(1024)}), f32[32768]{0:T(1024)}) %all-reduce.10.cloned.1.call-update) | async-done | bytes 131088 | tf_op jit(solution)/shard_map/while
  1190.4 1.0 reshape.118
  1193.8 259.2 %all-reduce.10.cloned.1.call-done = f32[32768]{0:T(1024)} async-done(((f32[32768]{0:T(1024)}), f32[32768]{0:T(1024)}) %all-reduce.10.cloned.1.call-update) | async-done | bytes 131088 | tf_op jit(solution)/shard_map/while
  1453.1 1.0 reshape.118
  1456.5 259.2 %all-reduce.10.cloned.1.call-done = f32[32768]{0:T(1024)} async-done(((f32[32768]{0:T(1024)}), f32[32768]{0:T(1024)}) %all-reduce.10.cloned.1.call-update) | async-done | bytes 131088 | tf_op jit(solution)/shard_map/while
  1715.8 1.0 reshape.118
  (256 shorter events, 26.0 us)
Async XLA Ops:
  7.2 48.6 %copy-start = (f32[24,24]{1,0:T(8,128)S(1)}, f32[24,24]{1,0:T(8,128)}, u32[]{:S(2)}) copy-start(f32[24,24]{1,0:T(8,128)} %param.14) | copy-start | bytes 6916
  7.2 16.8 copy-start.4
  8.0 16.1 collective-permute-start.1
  16.7 7.3 collective-permute-start
  20.7 10.3 collective-permute-start.4
  24.1 3.7 collective-permute-start.2
  26.4 4.5 collective-permute-start.3
  27.8 3.2 copy-start.54
  31.5 8.7 collective-permute-start.5
  49.9 8.5 copy-start.6
  55.8 2.7 copy-start.2
  69.4 2.7 copy-start.3
  74.4 4.7 copy-start.14
  74.4 4.7 copy-start.15
  74.4 4.8 copy-start.16
  74.4 4.8 copy-start.17
  74.4 4.8 copy-start.18
  74.4 4.8 copy-start.19
  74.4 4.8 copy-start.20
  74.4 4.8 copy-start.21
  74.4 4.8 copy-start.22
  74.4 4.8 copy-start.23
  74.5 4.8 copy-start.24
  75.4 3.8 copy-start.47
  75.4 3.9 copy-start.48
  75.4 3.9 copy-start.49
  75.4 3.9 copy-start.50
  75.4 3.9 copy-start.51
  75.4 3.9 copy-start.52
  83.9 4.5 copy-start.35
  83.9 4.5 copy-start.36
  83.9 4.5 copy-start.37
  83.9 4.5 copy-start.41
  83.9 4.5 copy-start.42
  83.9 4.5 copy-start.43
  83.9 4.5 copy-start.53
  93.7 22.6 %copy-start.58 = (f32[64]{0:T(128)S(1)}, f32[64]{0:T(128)}, u32[]{:S(2)}) copy-start(f32[64]{0:T(128)} %param.15) | copy-start | bytes 772
  95.0 10.3 collective-permute-start.6
  103.4 8.9 collective-permute-start.7
  112.3 4.1 collective-permute-start.8
  115.0 7.1 collective-permute-start.9
  122.9 1595.0 %copy-start.34 = (f32[8,8,128]{2,1,0:T(8,128)}, f32[8,8,128]{2,1,0:T(8,128)S(1)}, u32[]{:S(2)}) copy-start(f32[8,8,128]{2,1,0:T(8,128)S(1)} %get-tuple-element.101) | copy-start | bytes 98308
  123.0 278.7 %all-reduce.10.cloned.1.call-start = ((), (), s32[]{:S(2)}) async-start(), calls=%async_computation | async-start | bytes 262144 | tf_op jit(solution)/shard_map/while
  403.6 261.1 %all-reduce.10.cloned.1.call-start = ((), (), s32[]{:S(2)}) async-start(), calls=%async_computation | async-start | bytes 262144 | tf_op jit(solution)/shard_map/while
  666.6 261.1 %all-reduce.10.cloned.1.call-start = ((), (), s32[]{:S(2)}) async-start(), calls=%async_computation | async-start | bytes 262144 | tf_op jit(solution)/shard_map/while
  929.6 260.8 %all-reduce.10.cloned.1.call-start = ((), (), s32[]{:S(2)}) async-start(), calls=%async_computation | async-start | bytes 262144 | tf_op jit(solution)/shard_map/while
  1192.3 260.8 %all-reduce.10.cloned.1.call-start = ((), (), s32[]{:S(2)}) async-start(), calls=%async_computation | async-start | bytes 262144 | tf_op jit(solution)/shard_map/while
  1455.0 260.8 %all-reduce.10.cloned.1.call-start = ((), (), s32[]{:S(2)}) async-start(), calls=%async_computation | async-start | bytes 262144 | tf_op jit(solution)/shard_map/while
  (32 other events, 51.5 us)
Sparse Core Ops, SparseCore 0:
  128.8 272.8 all-reduce.9
  409.4 255.2 all-reduce.9
  672.4 255.2 all-reduce.9
  935.1 255.2 all-reduce.9
  1197.8 255.2 all-reduce.9
  1460.5 255.2 all-reduce.9
